TPU v7x, 32 devices: a whole 2x2x4 slice. The times are simulated.
32 devices in a mesh: grp: 2 (over y), tile: 4 (over z), freq: 4 (over x, core).
Axes of the slice: x: 2, y: 2, z: 4, core: 2. Of those that a mesh axis runs over, the one named last changes fastest.
Arguments:
- sources: bfloat16 [4, 4, 2048, 512], P('freq', 'grp', 'tile'), parts along dimension 1, may hold values from -6 to 6
- v_factors: bfloat16 [4, 4, 2, 4, 112, 512], P('freq', 'tile', None, 'grp'), parts along dimension 3, may hold values from -0.1875 to 0.1875
- u_factors: bfloat16 [4, 4, 4, 112, 1024], P('freq', None, 'grp', None, 'tile'), parts along dimension 2, may hold values from -0.1875 to 0.1875
- tile_ranks: int32 [4, 4, 4], P('freq', 'grp', 'tile'), parts along dimension 1, may hold values from 16 to 112, as said below
- window_bounds: int32 [4, 1024, 512], P('grp', ('tile', 'freq')), parts along dimension 0, may hold values from 0 to 31, as said below
Outputs:
- windowed_traces: float32 [1024, 64, 512], P(('tile', 'freq'), 'grp'), parts along dimension 1
There are 2 independent parts, one for each index of `grp`. A program takes and returns all parts, laid end to end along the dimension named above; each array names one. Nothing has to cross between parts.
Inputs may be any that keep to these rules, and one draw needn't show every extreme that they name: `tile_ranks`: each tile's rank for each frequency; rank slots at or beyond it carry no coefficients. window_bounds[1] - window_bounds[0] lies between 8 and 16 for every receiver and virtual source.
All inputs are finite; a program needn't handle non-finite values.
Results may differ from a plain program's by a relative error of at most 0.0041.
Values may be sent and summed in bfloat16 or wider, within the bound.
No kernel may reach another device: no remote copies, remote signals or barrier semaphores. Data moves between devices by JAX's collectives and lax.ppermute only.
A program may use at most 64 MiB of HBM per device.

v0:
```python
import math
import jax
import jax.numpy as jnp
from jax import lax
from jax.sharding import PartitionSpec as P

NT = 32
S_CHUNKS = 2
first_bin = 2


def inverse_tables(count_freq, count_time):
    freq_index = jnp.arange(count_freq, dtype=jnp.int32)[:, None] + first_bin
    time_index = jnp.arange(count_time, dtype=jnp.int32)[None, :]
    phase_step = freq_index * time_index % count_time
    angles = phase_step.astype(jnp.float32) * (2.0 * math.pi / count_time)
    return (jnp.cos(angles), jnp.sin(angles))


def column_products(v_local, x_local, rank_local):
    products = lax.dot_general(
        v_local, x_local, (((3,), (1,)), ((), ())), preferred_element_type=jnp.float32
    )
    coef_real = products[:, 0, :, 0] - products[:, 1, :, 1]
    coef_imag = products[:, 0, :, 1] + products[:, 1, :, 0]
    slot_index = jnp.arange(v_local.shape[2], dtype=jnp.int32)
    live_slots = slot_index[None, :, None] < rank_local[:, None, None]
    coef_real = jnp.where(live_slots, coef_real, jnp.float32(0.0)).astype(jnp.bfloat16)
    coef_imag = jnp.where(live_slots, coef_imag, jnp.float32(0.0)).astype(jnp.bfloat16)
    return jnp.stack([coef_real, coef_imag], axis=1)


def row_spectrum(u_local, blocks):
    products = lax.dot_general(
        u_local, blocks, (((0, 2), (0, 2)), ((), ())), preferred_element_type=jnp.float32
    )
    real_part = products[0, :, 0] - products[1, :, 1]
    imag_part = products[0, :, 1] + products[1, :, 0]
    return jnp.stack([real_part, imag_part], axis=0).astype(jnp.bfloat16)


def relay_exchange(own, u_local):
    t = lax.axis_index("tile")
    up = [(0, 1), (1, 2), (2, 3)]
    down = [(1, 0), (2, 1), (3, 2)]
    up1 = lax.ppermute(own[1], "tile", up)
    down1 = lax.ppermute(own[0], "tile", down)
    up2 = lax.ppermute(jnp.where(t == 0, own[0], up1), "tile", up)
    down2 = lax.ppermute(jnp.where(t == 3, own[1], down1), "tile", down)
    up3 = lax.ppermute(up2, "tile", [(2, 3)])
    down3 = lax.ppermute(down2, "tile", [(1, 0)])
    orders = (
        lambda: (own[0], down1, down2, down3),
        lambda: (up2, own[0], down1, down2),
        lambda: (up2, up1, own[1], down2),
        lambda: (up3, up2, up1, own[1]),
    )
    branches = [
        (lambda order: lambda: row_spectrum(u_local, jnp.stack(order(), axis=0)))(order)
        for order in orders
    ]
    return lax.switch(t, branches)


def gather_exchange(own, u_local, n_tile):
    repeat = n_tile // own.shape[0]
    sending = jnp.repeat(own, repeat, axis=0)
    received = lax.all_to_all(sending, "tile", split_axis=0, concat_axis=0, tiled=True)
    return row_spectrum(u_local, received)


def make_per_device(n_tile):

    def per_device(sources, v_factors, u_factors, tile_ranks, window_bounds):
        v_local = v_factors[0, 0]
        u_local = u_factors[0]
        x_local = sources[0]
        rank_local = tile_ranks[0, :, 0]
        rows = v_local.shape[0]
        use_relay = n_tile == 4 and rows == 2 and (u_local.shape[0] == 4)
        count_s = x_local.shape[2]
        chunks = S_CHUNKS if count_s % S_CHUNKS == 0 else 1
        width = count_s // chunks
        received_parts = []
        for c in range(chunks):
            x_part = x_local[:, :, c * width : (c + 1) * width]
            own = column_products(v_local, x_part, rank_local)
            if use_relay:
                spectrum = relay_exchange(own, u_local)
            else:
                spectrum = gather_exchange(own, u_local, n_tile)
            received_parts.append(
                lax.all_to_all(spectrum[None], "freq", split_axis=2, concat_axis=0, tiled=True)
            )
        received = jnp.concatenate(received_parts, axis=3) if chunks > 1 else received_parts[0]
        count_freq = received.shape[0]
        cosine_table, sine_table = inverse_tables(count_freq, NT)
        widened = received.astype(jnp.float32)
        real_sum = 0.0
        imag_sum = 0.0
        for f in range(count_freq):
            real_sum = real_sum + widened[f, 0][:, None, :] * cosine_table[f][None, :, None]
            imag_sum = imag_sum + widened[f, 1][:, None, :] * sine_table[f][None, :, None]
        traces = (real_sum - imag_sum) * (1.0 / math.sqrt(count_freq))
        time_index = jnp.arange(NT, dtype=jnp.int32)[None, :, None]
        inside = (time_index >= window_bounds[0][:, None, :]) & (
            time_index < window_bounds[1][:, None, :]
        )
        return jnp.where(inside, traces, jnp.float32(0.0))

    return per_device


def solution(mesh):
    return jax.shard_map(
        make_per_device(mesh.shape["tile"]),
        mesh=mesh,
        in_specs=(
            P("freq", "grp", "tile", None),
            P("freq", "tile", None, "grp", None, None),
            P("freq", None, "grp", None, "tile"),
            P("freq", "grp", "tile"),
            P("grp", ("tile", "freq"), None),
        ),
        out_specs=P(("tile", "freq"), "grp", None),
        check_vma=False,
    )
```

profile of v0, /device:TPU:0, one launch (start us, length us, event | category | flops | bytes accessed | tf_op | source)
XLA Modules:
  0.0 69.7 jit_solution(6855587100608741447)
XLA Ops:
  0.0 0.0 copy-start
  0.0 0.0 copy-start.2
  0.0 1.0 %copy-done = bf16[1,1,2,2,112,512]{5,4,3,2,1,0:T(8,128)(2,1)S(1)} copy-done((bf16[1,1,2,2,112,512]{5,4,3,2,1,0:T(8,128)(2,1)S(1)}, bf16[1,1,2,2,112,512]{5,4,3,2,1,0:T(8,128)(2,1)}, u32[]{:S(2)}) %copy-start) | copy-done | bytes 458776
  1.0 1.5 %fusion.90 = f32[2,2,112,2,256]{4,2,3,1,0:T(8,128)S(1)} fusion(bf16[2,512,512]{2,1,0:T(8,128)(2,1)} %bitcast.377, bf16[1,1,2,2,112,512]{5,4,3,2,1,0:T(8,128)(2,1)S(1)} %copy-done), kind=kOutput, calls=%fused_computation.143 | convolution fusion | flops 234881024 | bytes 1900544 | tf_op jit(solution)/shard_map/dot_general | solution.py:21
  2.5 1.4 %fusion.89 = f32[2,2,112,2,256]{4,2,0,3,1:T(8,128)S(1)} fusion(bf16[2,512,512]{2,1,0:T(8,128)(2,1)} %bitcast.378, bf16[1,1,2,2,112,512]{5,4,3,2,1,0:T(8,128)(2,1)S(1)} %copy-done), kind=kOutput, calls=%fused_computation.141 | convolution fusion | flops 234881024 | bytes 1900544 | tf_op jit(solution)/shard_map/dot_general | solution.py:21
  4.0 0.7 %iota_compare_fusion.2 = pred[2,112]{1,0:T(4,128)(4,1)S(1)} fusion(s32[2]{0:T(128)} %bitcast.408), kind=kLoop, calls=%fused_computation.207 | loop fusion | flops 224 | bytes 232 | tf_op jit(solution)/shard_map/lt | solution.py:27
  4.7 0.1 fusion.101
  4.8 0.1 fusion.98
  5.0 4.9 %collective-permute-start.3 = (bf16[2,112,256]{2,1,0:T(8,128)(2,1)S(1)}, bf16[2,112,256]{2,1,0:T(8,128)(2,1)S(1)}, u32[]{:S(2)}, u32[]{:S(2)}) collective-permute-start(bf16[2,112,256]{2,1,0:T(8,128)(2,1)S(1)} %fusion.114), channel_id=1, source_target_pairs={{0,4},{4,8},{8,12},{1,5},{5,9},{9,13},{2,6},{6,10},{10,14},{3,7},{... | collective-permute-start | bytes 344072 | tf_op jit(solution)/shard_map/ppermute | solution.py:46
  9.9 3.5 %collective-permute-start.9 = (bf16[2,112,256]{2,1,0:T(8,128)(2,1)S(1)}, bf16[2,112,256]{2,1,0:T(8,128)(2,1)S(1)}, u32[]{:S(2)}, u32[]{:S(2)}) collective-permute-start(bf16[2,112,256]{2,1,0:T(8,128)(2,1)S(1)} %fusion.110), channel_id=1, source_target_pairs={{0,4},{4,8},{8,12},{1,5},{5,9},{9,13},{2,6},{6,10},{10,14},{3,7},{... | collective-permute-start | bytes 344072 | tf_op jit(solution)/shard_map/ppermute | solution.py:46
  13.4 0.0 copy-done.2
  13.5 2.3 %collective-permute-done.9 = bf16[2,112,256]{2,1,0:T(8,128)(2,1)S(1)} collective-permute-done((bf16[2,112,256]{2,1,0:T(8,128)(2,1)S(1)}, bf16[2,112,256]{2,1,0:T(8,128)(2,1)S(1)}, u32[]{:S(2)}, u32[]{:S(2)}) %collective-permute-start.9) | collective-permute-done | bytes 114720 | tf_op jit(solution)/shard_map/ppermute | solution.py:46
  15.8 5.0 %collective-permute-start.10 = (bf16[2,112,256]{2,1,0:T(8,128)(2,1)S(1)}, bf16[2,112,256]{2,1,0:T(8,128)(2,1)}, u32[]{:S(2)}, u32[]{:S(2)}) collective-permute-start(bf16[2,112,256]{2,1,0:T(8,128)(2,1)S(1)} %get-tuple-element.201), channel_id=1, source_target_pairs={{0,4},{4,8},{8,12},{1,5},{5,9},{9,13},{2,6},{6,10},{10,14},{3,7},{... | collective-permute-start | bytes 344072 | tf_op jit(solution)/shard_map/ppermute | solution.py:48
  20.8 1.3 %collective-permute-start.6 = (bf16[2,112,256]{2,1,0:T(8,128)(2,1)S(1)}, bf16[2,112,256]{2,1,0:T(8,128)(2,1)S(1)}, u32[]{:S(2)}, u32[]{:S(2)}) collective-permute-start(bf16[2,112,256]{2,1,0:T(8,128)(2,1)S(1)} %get-tuple-element.202), channel_id=1, source_target_pairs={{4,0},{8,4},{12,8},{5,1},{9,5},{13,9},{6,2},{10,6},{14,10},{7,3},{... | collective-permute-start | bytes 344072 | tf_op jit(solution)/shard_map/ppermute | solution.py:47
  22.1 0.0 collective-permute-done.3
  22.1 1.3 %collective-permute-start = (bf16[2,112,256]{2,1,0:T(8,128)(2,1)S(1)}, bf16[2,112,256]{2,1,0:T(8,128)(2,1)S(1)}, u32[]{:S(2)}, u32[]{:S(2)}) collective-permute-start(bf16[2,112,256]{2,1,0:T(8,128)(2,1)S(1)} %get-tuple-element.200), channel_id=1, source_target_pairs={{4,0},{8,4},{12,8},{5,1},{9,5},{13,9},{6,2},{10,6},{14,10},{7,3},{... | collective-permute-start | bytes 344072 | tf_op jit(solution)/shard_map/ppermute | solution.py:47
  23.4 4.4 %collective-permute-done.6 = bf16[2,112,256]{2,1,0:T(8,128)(2,1)S(1)} collective-permute-done((bf16[2,112,256]{2,1,0:T(8,128)(2,1)S(1)}, bf16[2,112,256]{2,1,0:T(8,128)(2,1)S(1)}, u32[]{:S(2)}, u32[]{:S(2)}) %collective-permute-start.6) | collective-permute-done | bytes 114720 | tf_op jit(solution)/shard_map/ppermute | solution.py:47
  27.8 1.3 %collective-permute-start.7 = (bf16[2,112,256]{2,1,0:T(8,128)(2,1)S(1)}, bf16[2,112,256]{2,1,0:T(8,128)(2,1)S(1)}, u32[]{:S(2)}, u32[]{:S(2)}) collective-permute-start(bf16[2,112,256]{2,1,0:T(8,128)(2,1)S(1)} %broadcast_select_fusion.2), channel_id=1, source_target_pairs={{4,0},{8,4},{12,8},{5,1},{9,5},{13,9},{6,2},{10,6},{14,10},{7,3},{... | collective-permute-start | bytes 344072 | tf_op jit(solution)/shard_map/ppermute | solution.py:49
  29.1 0.0 copy-done.1
  29.2 4.6 %collective-permute-start.4 = (bf16[2,112,256]{2,1,0:T(8,128)(2,1)S(1)}, bf16[2,112,256]{2,1,0:T(8,128)(2,1)S(1)}, u32[]{:S(2)}, u32[]{:S(2)}) collective-permute-start(bf16[2,112,256]{2,1,0:T(8,128)(2,1)S(1)} %get-tuple-element.199), channel_id=1, source_target_pairs={{0,4},{4,8},{8,12},{1,5},{5,9},{9,13},{2,6},{6,10},{10,14},{3,7},{... | collective-permute-start | bytes 344072 | tf_op jit(solution)/shard_map/ppermute | solution.py:48
  33.8 0.0 collective-permute-done.10
  33.8 0.7 collective-permute-start.11
  34.5 0.0 collective-permute-done.7
  34.5 1.3 %collective-permute-start.8 = (bf16[2,112,256]{2,1,0:T(8,128)(2,1)S(1)}, bf16[2,112,256]{2,1,0:T(8,128)(2,1)S(1)}, u32[]{:S(2)}, u32[]{:S(2)}) collective-permute-start(bf16[2,112,256]{2,1,0:T(8,128)(2,1)S(1)} %collective-permute-done.7), channel_id=1, source_target_pairs={{4,0},{5,1},{6,2},{7,3},{20,16},{21,17},{22,18},{23,19}} | collective-permute-start | bytes 344072 | tf_op jit(solution)/shard_map/ppermute | solution.py:51
  35.8 0.0 collective-permute-done
  35.8 1.3 %collective-permute-start.1 = (bf16[2,112,256]{2,1,0:T(8,128)(2,1)S(1)}, bf16[2,112,256]{2,1,0:T(8,128)(2,1)S(1)}, u32[]{:S(2)}, u32[]{:S(2)}) collective-permute-start(bf16[2,112,256]{2,1,0:T(8,128)(2,1)S(1)} %broadcast_select_fusion.3), channel_id=1, source_target_pairs={{4,0},{8,4},{12,8},{5,1},{9,5},{13,9},{6,2},{10,6},{14,10},{7,3},{... | collective-permute-start | bytes 344072 | tf_op jit(solution)/shard_map/ppermute | solution.py:49
  37.1 0.0 collective-permute-done.11
  37.1 4.0 %collective-permute-done.8 = bf16[2,112,256]{2,1,0:T(8,128)(2,1)S(1)} collective-permute-done((bf16[2,112,256]{2,1,0:T(8,128)(2,1)S(1)}, bf16[2,112,256]{2,1,0:T(8,128)(2,1)S(1)}, u32[]{:S(2)}, u32[]{:S(2)}) %collective-permute-start.8) | collective-permute-done | bytes 114720 | tf_op jit(solution)/shard_map/ppermute | solution.py:51
  41.2 0.6 conditional.5
  41.2 0.5 convolution_bitcast_fusion.4
  41.8 0.9 %copy.148 = bf16[2,256,256]{2,0,1:T(2,128)(2,1)} copy(bf16[2,256,256]{1,2,0:T(8,128)(2,1)S(1)} %get-tuple-element.231) | data formatting | bytes 524288
  42.7 3.4 %all-to-all-start.1 = ((bf16[1,2,256,256]{3,1,0,2:T(2,128)(2,1)}), bf16[1,2,256,256]{3,1,0,2:T(2,128)(2,1)S(1)}, u32[]{:S(2)}, u32[]{:S(2)}) async-start(bf16[1,2,256,256]{3,1,0,2:T(2,128)(2,1)} %bitcast.124), calls=%async_computation.1 | async-start | bytes 524288 | tf_op jit(solution)/shard_map/all_to_all | solution.py:93
  46.1 0.1 fusion.119
  46.2 0.0 collective-permute-done.4
  46.2 0.7 collective-permute-start.5
  46.9 0.0 collective-permute-done.1
  46.9 1.3 %collective-permute-start.2 = (bf16[2,112,256]{2,1,0:T(8,128)(2,1)S(1)}, bf16[2,112,256]{2,1,0:T(8,128)(2,1)S(1)}, u32[]{:S(2)}, u32[]{:S(2)}) collective-permute-start(bf16[2,112,256]{2,1,0:T(8,128)(2,1)S(1)} %collective-permute-done.1), channel_id=1, source_target_pairs={{4,0},{5,1},{6,2},{7,3},{20,16},{21,17},{22,18},{23,19}} | collective-permute-start | bytes 344072 | tf_op jit(solution)/shard_map/ppermute | solution.py:51
  48.2 0.0 collective-permute-done.5
  48.2 6.1 %collective-permute-done.2 = bf16[2,112,256]{2,1,0:T(8,128)(2,1)S(1)} collective-permute-done((bf16[2,112,256]{2,1,0:T(8,128)(2,1)S(1)}, bf16[2,112,256]{2,1,0:T(8,128)(2,1)S(1)}, u32[]{:S(2)}, u32[]{:S(2)}) %collective-permute-start.2) | collective-permute-done | bytes 114720 | tf_op jit(solution)/shard_map/ppermute | solution.py:51
  54.3 0.6 conditional.4
  54.3 0.5 convolution_bitcast_fusion
  54.9 0.9 %copy.147 = bf16[2,256,256]{2,0,1:T(2,128)(2,1)} copy(bf16[2,256,256]{1,2,0:T(8,128)(2,1)S(1)} %get-tuple-element.230) | data formatting | bytes 524288
  55.8 0.0 all-to-all-done.1
  55.8 3.4 %all-to-all-start = ((bf16[1,2,256,256]{3,1,0,2:T(2,128)(2,1)}), bf16[1,2,256,256]{3,1,0,2:T(2,128)(2,1)S(1)}, u32[]{:S(2)}, u32[]{:S(2)}) async-start(bf16[1,2,256,256]{3,1,0,2:T(2,128)(2,1)} %bitcast.113), calls=%async_computation | async-start | bytes 524288 | tf_op jit(solution)/shard_map/all_to_all | solution.py:93
  59.2 5.9 %all-to-all-done = bf16[1,2,256,256]{3,1,0,2:T(2,128)(2,1)S(1)} async-done(((bf16[1,2,256,256]{3,1,0,2:T(2,128)(2,1)}), bf16[1,2,256,256]{3,1,0,2:T(2,128)(2,1)S(1)}, u32[]{:S(2)}, u32[]{:S(2)}) %all-to-all-start) | async-done | bytes 262176 | tf_op jit(solution)/shard_map/all_to_all | solution.py:93
  65.2 0.1 maximum_convert_fusion
  65.3 0.1 slice_bitcast_fusion.29
  65.4 4.3 %multiply_select_fusion = f32[64,32,512]{2,1,0:T(8,128)} fusion(f32[32]{0:T(128)S(1)} %get-tuple-element.220, f32[64,512]{1,0:T(8,128)S(1)} %get-tuple-element.204, f32[32]{0:T(128)S(1)} %get-tuple-element.221, f32[64,512]{1,0:T(8,128)S(1)} %get-tuple-element.205, f32[32]{0:T(128)S(1)} %get-tuple-element.222, f32[64,512]{1,0:T(8,128)S(1)} %get-tuple-element.206, ...), kind=kLoop, calls=%fused_computation.136 | loop fusion | flops 20971520 | bytes 5506048 | tf_op jit(solution)/shard_map/jit(_where)/select_n | solution.py:109
  (24 shorter events, 0.5 us)
Async XLA Ops:
  0.0 1.0 %copy-start = (bf16[1,1,2,2,112,512]{5,4,3,2,1,0:T(8,128)(2,1)S(1)}, bf16[1,1,2,2,112,512]{5,4,3,2,1,0:T(8,128)(2,1)}, u32[]{:S(2)}) copy-start(bf16[1,1,2,2,112,512]{5,4,3,2,1,0:T(8,128)(2,1)} %param.14) | copy-start | bytes 1376260
  0.0 13.4 %copy-start.2 = (s32[2,64,512]{2,1,0:T(8,128)S(1)}, s32[2,64,512]{2,1,0:T(8,128)}, u32[]{:S(2)}) copy-start(s32[2,64,512]{2,1,0:T(8,128)} %param.17) | copy-start | bytes 786436
  1.0 28.1 %copy-start.1 = (bf16[1,4,2,112,256]{4,3,2,1,0:T(8,128)(2,1)S(1)}, bf16[1,4,2,112,256]{4,3,2,1,0:T(8,128)(2,1)}, u32[]{:S(2)}) copy-start(bf16[1,4,2,112,256]{4,3,2,1,0:T(8,128)(2,1)} %param.15) | copy-start | bytes 1376260
  5.0 17.1 %collective-permute-start.3 = (bf16[2,112,256]{2,1,0:T(8,128)(2,1)S(1)}, bf16[2,112,256]{2,1,0:T(8,128)(2,1)S(1)}, u32[]{:S(2)}, u32[]{:S(2)}) collective-permute-start(bf16[2,112,256]{2,1,0:T(8,128)(2,1)S(1)} %fusion.114), channel_id=1, source_target_pairs={{0,4},{4,8},{8,12},{1,5},{5,9},{9,13},{2,6},{6,10},{10,14},{3,7},{... | collective-permute-start | bytes 344072 | tf_op jit(solution)/shard_map/ppermute | solution.py:46
  9.9 5.8 %collective-permute-start.9 = (bf16[2,112,256]{2,1,0:T(8,128)(2,1)S(1)}, bf16[2,112,256]{2,1,0:T(8,128)(2,1)S(1)}, u32[]{:S(2)}, u32[]{:S(2)}) collective-permute-start(bf16[2,112,256]{2,1,0:T(8,128)(2,1)S(1)} %fusion.110), channel_id=1, source_target_pairs={{0,4},{4,8},{8,12},{1,5},{5,9},{9,13},{2,6},{6,10},{10,14},{3,7},{... | collective-permute-start | bytes 344072 | tf_op jit(solution)/shard_map/ppermute | solution.py:46
  15.8 18.0 %collective-permute-start.10 = (bf16[2,112,256]{2,1,0:T(8,128)(2,1)S(1)}, bf16[2,112,256]{2,1,0:T(8,128)(2,1)}, u32[]{:S(2)}, u32[]{:S(2)}) collective-permute-start(bf16[2,112,256]{2,1,0:T(8,128)(2,1)S(1)} %get-tuple-element.201), channel_id=1, source_target_pairs={{0,4},{4,8},{8,12},{1,5},{5,9},{9,13},{2,6},{6,10},{10,14},{3,7},{... | collective-permute-start | bytes 344072 | tf_op jit(solution)/shard_map/ppermute | solution.py:48
  20.8 7.0 %collective-permute-start.6 = (bf16[2,112,256]{2,1,0:T(8,128)(2,1)S(1)}, bf16[2,112,256]{2,1,0:T(8,128)(2,1)S(1)}, u32[]{:S(2)}, u32[]{:S(2)}) collective-permute-start(bf16[2,112,256]{2,1,0:T(8,128)(2,1)S(1)} %get-tuple-element.202), channel_id=1, source_target_pairs={{4,0},{8,4},{12,8},{5,1},{9,5},{13,9},{6,2},{10,6},{14,10},{7,3},{... | collective-permute-start | bytes 344072 | tf_op jit(solution)/shard_map/ppermute | solution.py:47
  22.1 13.7 %collective-permute-start = (bf16[2,112,256]{2,1,0:T(8,128)(2,1)S(1)}, bf16[2,112,256]{2,1,0:T(8,128)(2,1)S(1)}, u32[]{:S(2)}, u32[]{:S(2)}) collective-permute-start(bf16[2,112,256]{2,1,0:T(8,128)(2,1)S(1)} %get-tuple-element.200), channel_id=1, source_target_pairs={{4,0},{8,4},{12,8},{5,1},{9,5},{13,9},{6,2},{10,6},{14,10},{7,3},{... | collective-permute-start | bytes 344072 | tf_op jit(solution)/shard_map/ppermute | solution.py:47
  27.8 6.7 %collective-permute-start.7 = (bf16[2,112,256]{2,1,0:T(8,128)(2,1)S(1)}, bf16[2,112,256]{2,1,0:T(8,128)(2,1)S(1)}, u32[]{:S(2)}, u32[]{:S(2)}) collective-permute-start(bf16[2,112,256]{2,1,0:T(8,128)(2,1)S(1)} %broadcast_select_fusion.2), channel_id=1, source_target_pairs={{4,0},{8,4},{12,8},{5,1},{9,5},{13,9},{6,2},{10,6},{14,10},{7,3},{... | collective-permute-start | bytes 344072 | tf_op jit(solution)/shard_map/ppermute | solution.py:49
  29.2 17.0 %collective-permute-start.4 = (bf16[2,112,256]{2,1,0:T(8,128)(2,1)S(1)}, bf16[2,112,256]{2,1,0:T(8,128)(2,1)S(1)}, u32[]{:S(2)}, u32[]{:S(2)}) collective-permute-start(bf16[2,112,256]{2,1,0:T(8,128)(2,1)S(1)} %get-tuple-element.199), channel_id=1, source_target_pairs={{0,4},{4,8},{8,12},{1,5},{5,9},{9,13},{2,6},{6,10},{10,14},{3,7},{... | collective-permute-start | bytes 344072 | tf_op jit(solution)/shard_map/ppermute | solution.py:48
  33.8 3.3 %collective-permute-start.11 = (bf16[2,112,256]{2,1,0:T(8,128)(2,1)}, bf16[2,112,256]{2,1,0:T(8,128)(2,1)S(1)}, u32[]{:S(2)}, u32[]{:S(2)}) collective-permute-start(bf16[2,112,256]{2,1,0:T(8,128)(2,1)} %collective-permute-done.10), channel_id=1, source_target_pairs={{8,12},{9,13},{10,14},{11,15},{24,28},{25,29},{26,30},{27,31}} | collective-permute-start | bytes 344072 | tf_op jit(solution)/shard_map/ppermute | solution.py:50
  34.5 6.7 %collective-permute-start.8 = (bf16[2,112,256]{2,1,0:T(8,128)(2,1)S(1)}, bf16[2,112,256]{2,1,0:T(8,128)(2,1)S(1)}, u32[]{:S(2)}, u32[]{:S(2)}) collective-permute-start(bf16[2,112,256]{2,1,0:T(8,128)(2,1)S(1)} %collective-permute-done.7), channel_id=1, source_target_pairs={{4,0},{5,1},{6,2},{7,3},{20,16},{21,17},{22,18},{23,19}} | collective-permute-start | bytes 344072 | tf_op jit(solution)/shard_map/ppermute | solution.py:51
  35.8 11.1 %collective-permute-start.1 = (bf16[2,112,256]{2,1,0:T(8,128)(2,1)S(1)}, bf16[2,112,256]{2,1,0:T(8,128)(2,1)S(1)}, u32[]{:S(2)}, u32[]{:S(2)}) collective-permute-start(bf16[2,112,256]{2,1,0:T(8,128)(2,1)S(1)} %broadcast_select_fusion.3), channel_id=1, source_target_pairs={{4,0},{8,4},{12,8},{5,1},{9,5},{13,9},{6,2},{10,6},{14,10},{7,3},{... | collective-permute-start | bytes 344072 | tf_op jit(solution)/shard_map/ppermute | solution.py:49
  42.7 13.1 %all-to-all-start.1 = ((bf16[1,2,256,256]{3,1,0,2:T(2,128)(2,1)}), bf16[1,2,256,256]{3,1,0,2:T(2,128)(2,1)S(1)}, u32[]{:S(2)}, u32[]{:S(2)}) async-start(bf16[1,2,256,256]{3,1,0,2:T(2,128)(2,1)} %bitcast.124), calls=%async_computation.1 | async-start | bytes 524288 | tf_op jit(solution)/shard_map/all_to_all | solution.py:93
  46.2 2.0 %collective-permute-start.5 = (bf16[2,112,256]{2,1,0:T(8,128)(2,1)S(1)}, bf16[2,112,256]{2,1,0:T(8,128)(2,1)S(1)}, u32[]{:S(2)}, u32[]{:S(2)}) collective-permute-start(bf16[2,112,256]{2,1,0:T(8,128)(2,1)S(1)} %collective-permute-done.4), channel_id=1, source_target_pairs={{8,12},{9,13},{10,14},{11,15},{24,28},{25,29},{26,30},{27,31}} | collective-permute-start | bytes 344072 | tf_op jit(solution)/shard_map/ppermute | solution.py:50
  46.9 7.4 %collective-permute-start.2 = (bf16[2,112,256]{2,1,0:T(8,128)(2,1)S(1)}, bf16[2,112,256]{2,1,0:T(8,128)(2,1)S(1)}, u32[]{:S(2)}, u32[]{:S(2)}) collective-permute-start(bf16[2,112,256]{2,1,0:T(8,128)(2,1)S(1)} %collective-permute-done.1), channel_id=1, source_target_pairs={{4,0},{5,1},{6,2},{7,3},{20,16},{21,17},{22,18},{23,19}} | collective-permute-start | bytes 344072 | tf_op jit(solution)/shard_map/ppermute | solution.py:51
  55.8 9.4 %all-to-all-start = ((bf16[1,2,256,256]{3,1,0,2:T(2,128)(2,1)}), bf16[1,2,256,256]{3,1,0,2:T(2,128)(2,1)S(1)}, u32[]{:S(2)}, u32[]{:S(2)}) async-start(bf16[1,2,256,256]{3,1,0,2:T(2,128)(2,1)} %bitcast.113), calls=%async_computation | async-start | bytes 524288 | tf_op jit(solution)/shard_map/all_to_all | solution.py:93
where the time goes:
time: 70.3 us; the launch traced here: 69.7 us
  starting transfers between devices  33.8 us (48%)
  waiting for transfers between devices  22.8 us (32%)
  other arithmetic  5.77 us (8%)
  matrix products  3.87 us (6%)
  local copies, waits for them, and re-layouts  2.97 us (4%)
    ppermute x2, waiting for transfers between devices, relay_exchange(): down3 = lax.ppermute(down2, 'tile', [(1, 0)])  10.1 us
    ppermute x2, starting transfers between devices, relay_exchange(): up2 = lax.ppermute(jnp.where(t == 0, own[0], up1), 'tile', up)  9.53 us
    ppermute x2, starting transfers between devices, relay_exchange(): up1 = lax.ppermute(own[1], 'tile', up)  8.42 us
    all_to_all x2, starting transfers between devices, per_device(): lax.all_to_all(spectrum[None], 'freq', split_axis=2, concat_axis=0, tiled...  6.81 us
    all_to_all x2, waiting for transfers between devices, per_device(): lax.all_to_all(spectrum[None], 'freq', split_axis=2, concat_axis=0, tiled...  5.95 us
    ppermute x2, waiting for transfers between devices, relay_exchange(): down1 = lax.ppermute(own[0], 'tile', down)  4.4 us
    select_n x1, other arithmetic, per_device(): return jnp.where(inside, traces, jnp.float32(0.0))  4.26 us
    dot_general x2, matrix products, column_products(): lax.dot_general(v_local, x_local, (((3,), (1,)), ((), ())), preferred_ele...  2.94 us
  transfers between devices with their start and end apart: 14, of which 5 were waited for; matrix products, arithmetic and copies ran while one was open for 5% of the time, Pallas kernels for 0%

commit v1 on v0

--- a/solution.py
+++ b/solution.py
@@ -7,6 +7,22 @@
 NT = 32
 S_CHUNKS = 2
 first_bin = 2
+
+
+def exchange_in_pairs(x, axis, split, join):
+    ways, here = (lax.axis_size(axis), lax.axis_index(axis))
+    width = x.shape[split] // ways
+    shape = list(x.shape)
+    shape[split] = width
+    height = shape[join]
+    shape[join] = height * ways
+    full = jnp.zeros(shape, x.dtype)
+    for mask in range(ways):
+        part = lax.dynamic_slice_in_dim(x, (here ^ mask) * width, width, axis=split)
+        if mask:
+            part = lax.ppermute(part, axis, [(d, d ^ mask) for d in range(ways)])
+        full = lax.dynamic_update_slice_in_dim(full, part, (here ^ mask) * height, axis=join)
+    return full
 
 
 def inverse_tables(count_freq, count_time):
@@ -89,9 +105,7 @@
                 spectrum = relay_exchange(own, u_local)
             else:
                 spectrum = gather_exchange(own, u_local, n_tile)
-            received_parts.append(
-                lax.all_to_all(spectrum[None], "freq", split_axis=2, concat_axis=0, tiled=True)
-            )
+            received_parts.append(exchange_in_pairs(spectrum[None], "freq", 2, 0))
         received = jnp.concatenate(received_parts, axis=3) if chunks > 1 else received_parts[0]
         count_freq = received.shape[0]
         cosine_table, sine_table = inverse_tables(count_freq, NT)

time: 70.3 us -> 57.6 us (0.82)
  waiting for transfers between devices: 22.8 us -> 15.1 us
  starting transfers between devices: 33.8 us -> 30.3 us
  local copies, waits for them, and re-layouts: 2.97 us -> 1.63 us
    ppermute x2, waiting for transfers between devices: 10.1 us -> 2.63 us  [relay_exchange(): down3 = lax.ppermute(down2, 'tile', [(1, 0)])]
    all_to_all x2 -> x0, starting transfers between devices: 6.81 us -> none  [per_device(): lax.all_to_all(spectrum[None], 'freq', split_axis=2, concat_axis=0, tiled...]
    all_to_all x2 -> x0, waiting for transfers between devices: 5.95 us -> none  [per_device(): lax.all_to_all(spectrum[None], 'freq', split_axis=2, concat_axis=0, tiled...]
    ppermute x0 -> x6, starting transfers between devices: none -> 3.91 us  [exchange_in_pairs(): part = lax.ppermute(part, axis, [(d, d ^ mask) for d in range(ways)])]
    ppermute x0 -> x6, waiting for transfers between devices: none -> 3.72 us  [exchange_in_pairs(): part = lax.ppermute(part, axis, [(d, d ^ mask) for d in range(ways)])]
    ppermute x2, waiting for transfers between devices: 0.04 us -> 2.69 us  [relay_exchange(): down2 = lax.ppermute(jnp.where(t == 3, own[1], down1), 'tile', down)]
    unnamed x9 -> x7, local copies, waits for them, and re-layouts: 2.78 us -> 1.05 us
  transfers between devices with their start and end apart: 14 -> 18, of which waited for: 5 -> 8; matrix products, arithmetic and copies ran while one was open for 5% -> 3% of each run, Pallas kernels for 0% -> 0%
where the time goes in v1:
time: 57.6 us; the launch traced here: 57.2 us
  starting transfers between devices  30.3 us (53%)
  waiting for transfers between devices  15.1 us (26%)
  other arithmetic  5.77 us (10%)
  matrix products  3.81 us (7%)
  local copies, waits for them, and re-layouts  1.63 us (3%)
    ppermute x2, starting transfers between devices, relay_exchange(): up2 = lax.ppermute(jnp.where(t == 0, own[0], up1), 'tile', up)  8.89 us
    ppermute x2, starting transfers between devices, relay_exchange(): up1 = lax.ppermute(own[1], 'tile', up)  8.42 us
    select_n x1, other arithmetic, per_device(): return jnp.where(inside, traces, jnp.float32(0.0))  4.26 us
    ppermute x2, waiting for transfers between devices, relay_exchange(): down1 = lax.ppermute(own[0], 'tile', down)  4.05 us
    ppermute x6, starting transfers between devices, exchange_in_pairs(): part = lax.ppermute(part, axis, [(d, d ^ mask) for d in range(ways)])  3.91 us
    ppermute x6, waiting for transfers between devices, exchange_in_pairs(): part = lax.ppermute(part, axis, [(d, d ^ mask) for d in range(ways)])  3.72 us
    dot_general x2, matrix products, column_products(): lax.dot_general(v_local, x_local, (((3,), (1,)), ((), ())), preferred_ele...  2.88 us
    ppermute x2, waiting for transfers between devices, relay_exchange(): down2 = lax.ppermute(jnp.where(t == 3, own[1], down1), 'tile', down)  2.69 us
  transfers between devices with their start and end apart: 18, of which 8 were waited for; matrix products, arithmetic and copies ran while one was open for 3% of the time, Pallas kernels for 0%

profile of v1, /device:TPU:0, one launch (start us, length us, event | category | flops | bytes accessed | tf_op | source)
XLA Modules:
  0.0 57.2 jit_solution(7938756563808510828)
XLA Ops:
  0.0 1.0 %copy-done = bf16[1,1,2,2,112,512]{5,4,3,2,1,0:T(8,128)(2,1)S(1)} copy-done((bf16[1,1,2,2,112,512]{5,4,3,2,1,0:T(8,128)(2,1)S(1)}, bf16[1,1,2,2,112,512]{5,4,3,2,1,0:T(8,128)(2,1)}, u32[]{:S(2)}) %copy-start) | copy-done | bytes 458776
  1.0 1.4 %fusion.106 = f32[2,2,112,2,256]{4,2,3,1,0:T(8,128)S(1)} fusion(bf16[2,512,512]{2,1,0:T(8,128)(2,1)} %bitcast.411, bf16[1,1,2,2,112,512]{5,4,3,2,1,0:T(8,128)(2,1)S(1)} %copy-done), kind=kOutput, calls=%fused_computation.159 | convolution fusion | flops 234881024 | bytes 1900544 | tf_op jit(solution)/shard_map/dot_general | solution.py:37
  2.5 1.4 %fusion.105 = f32[2,2,112,2,256]{4,2,0,3,1:T(8,128)S(1)} fusion(bf16[2,512,512]{2,1,0:T(8,128)(2,1)} %bitcast.412, bf16[1,1,2,2,112,512]{5,4,3,2,1,0:T(8,128)(2,1)S(1)} %copy-done), kind=kOutput, calls=%fused_computation.157 | convolution fusion | flops 234881024 | bytes 1900544 | tf_op jit(solution)/shard_map/dot_general | solution.py:37
  3.9 0.7 %iota_compare_fusion.2 = pred[2,112]{1,0:T(4,128)(4,1)S(1)} fusion(s32[2]{0:T(128)} %bitcast.445), kind=kLoop, calls=%fused_computation.237 | loop fusion | flops 224 | bytes 232 | tf_op jit(solution)/shard_map/lt | solution.py:43
  4.6 0.1 fusion.117
  4.7 0.1 fusion.114
  4.9 4.9 %collective-permute-start.3 = (bf16[2,112,256]{2,1,0:T(8,128)(2,1)S(1)}, bf16[2,112,256]{2,1,0:T(8,128)(2,1)S(1)}, u32[]{:S(2)}, u32[]{:S(2)}) collective-permute-start(bf16[2,112,256]{2,1,0:T(8,128)(2,1)S(1)} %fusion.130), channel_id=1, source_target_pairs={{0,4},{4,8},{8,12},{1,5},{5,9},{9,13},{2,6},{6,10},{10,14},{3,7},{... | collective-permute-start | bytes 344072 | tf_op jit(solution)/shard_map/ppermute | solution.py:62
  9.9 3.5 %collective-permute-start.12 = (bf16[2,112,256]{2,1,0:T(8,128)(2,1)S(1)}, bf16[2,112,256]{2,1,0:T(8,128)(2,1)S(1)}, u32[]{:S(2)}, u32[]{:S(2)}) collective-permute-start(bf16[2,112,256]{2,1,0:T(8,128)(2,1)S(1)} %fusion.126), channel_id=1, source_target_pairs={{0,4},{4,8},{8,12},{1,5},{5,9},{9,13},{2,6},{6,10},{10,14},{3,7},{... | collective-permute-start | bytes 344072 | tf_op jit(solution)/shard_map/ppermute | solution.py:62
  13.4 0.1 fusion.135
  13.7 2.0 %collective-permute-done.12 = bf16[2,112,256]{2,1,0:T(8,128)(2,1)S(1)} collective-permute-done((bf16[2,112,256]{2,1,0:T(8,128)(2,1)S(1)}, bf16[2,112,256]{2,1,0:T(8,128)(2,1)S(1)}, u32[]{:S(2)}, u32[]{:S(2)}) %collective-permute-start.12) | collective-permute-done | bytes 114720 | tf_op jit(solution)/shard_map/ppermute | solution.py:62
  15.7 4.3 %collective-permute-start.13 = (bf16[2,112,256]{2,1,0:T(8,128)(2,1)S(1)}, bf16[2,112,256]{2,1,0:T(8,128)(2,1)S(1)}, u32[]{:S(2)}, u32[]{:S(2)}) collective-permute-start(bf16[2,112,256]{2,1,0:T(8,128)(2,1)S(1)} %get-tuple-element.191), channel_id=1, source_target_pairs={{0,4},{4,8},{8,12},{1,5},{5,9},{9,13},{2,6},{6,10},{10,14},{3,7},{... | collective-permute-start | bytes 344072 | tf_op jit(solution)/shard_map/ppermute | solution.py:64
  20.1 1.3 %collective-permute-start.9 = (bf16[2,112,256]{2,1,0:T(8,128)(2,1)S(1)}, bf16[2,112,256]{2,1,0:T(8,128)(2,1)S(1)}, u32[]{:S(2)}, u32[]{:S(2)}) collective-permute-start(bf16[2,112,256]{2,1,0:T(8,128)(2,1)S(1)} %get-tuple-element.192), channel_id=1, source_target_pairs={{4,0},{8,4},{12,8},{5,1},{9,5},{13,9},{6,2},{10,6},{14,10},{7,3},{... | collective-permute-start | bytes 344072 | tf_op jit(solution)/shard_map/ppermute | solution.py:63
  21.4 0.0 collective-permute-done.3
  21.4 4.6 %collective-permute-start.4 = (bf16[2,112,256]{2,1,0:T(8,128)(2,1)S(1)}, bf16[2,112,256]{2,1,0:T(8,128)(2,1)S(1)}, u32[]{:S(2)}, u32[]{:S(2)}) collective-permute-start(bf16[2,112,256]{2,1,0:T(8,128)(2,1)S(1)} %get-tuple-element.189), channel_id=1, source_target_pairs={{0,4},{4,8},{8,12},{1,5},{5,9},{9,13},{2,6},{6,10},{10,14},{3,7},{... | collective-permute-start | bytes 344072 | tf_op jit(solution)/shard_map/ppermute | solution.py:64
  26.0 1.3 %collective-permute-start = (bf16[2,112,256]{2,1,0:T(8,128)(2,1)S(1)}, bf16[2,112,256]{2,1,0:T(8,128)(2,1)S(1)}, u32[]{:S(2)}, u32[]{:S(2)}) collective-permute-start(bf16[2,112,256]{2,1,0:T(8,128)(2,1)S(1)} %get-tuple-element.190), channel_id=1, source_target_pairs={{4,0},{8,4},{12,8},{5,1},{9,5},{13,9},{6,2},{10,6},{14,10},{7,3},{... | collective-permute-start | bytes 344072 | tf_op jit(solution)/shard_map/ppermute | solution.py:63
  27.3 0.0 collective-permute-done.9
  27.3 1.3 %collective-permute-start.10 = (bf16[2,112,256]{2,1,0:T(8,128)(2,1)S(1)}, bf16[2,112,256]{2,1,0:T(8,128)(2,1)S(1)}, u32[]{:S(2)}, u32[]{:S(2)}) collective-permute-start(bf16[2,112,256]{2,1,0:T(8,128)(2,1)S(1)} %broadcast_select_fusion.2), channel_id=1, source_target_pairs={{4,0},{8,4},{12,8},{5,1},{9,5},{13,9},{6,2},{10,6},{14,10},{7,3},{... | collective-permute-start | bytes 344072 | tf_op jit(solution)/shard_map/ppermute | solution.py:65
  28.6 4.1 %collective-permute-done = bf16[2,112,256]{2,1,0:T(8,128)(2,1)S(1)} collective-permute-done((bf16[2,112,256]{2,1,0:T(8,128)(2,1)S(1)}, bf16[2,112,256]{2,1,0:T(8,128)(2,1)S(1)}, u32[]{:S(2)}, u32[]{:S(2)}) %collective-permute-start) | collective-permute-done | bytes 114720 | tf_op jit(solution)/shard_map/ppermute | solution.py:63
  32.7 1.3 %collective-permute-start.1 = (bf16[2,112,256]{2,1,0:T(8,128)(2,1)S(1)}, bf16[2,112,256]{2,1,0:T(8,128)(2,1)S(1)}, u32[]{:S(2)}, u32[]{:S(2)}) collective-permute-start(bf16[2,112,256]{2,1,0:T(8,128)(2,1)S(1)} %broadcast_select_fusion.3), channel_id=1, source_target_pairs={{4,0},{8,4},{12,8},{5,1},{9,5},{13,9},{6,2},{10,6},{14,10},{7,3},{... | collective-permute-start | bytes 344072 | tf_op jit(solution)/shard_map/ppermute | solution.py:65
  34.0 0.0 collective-permute-done.13
  34.0 0.7 %collective-permute-start.14 = (bf16[2,112,256]{2,1,0:T(8,128)(2,1)S(1)}, bf16[2,112,256]{2,1,0:T(8,128)(2,1)S(1)}, u32[]{:S(2)}, u32[]{:S(2)}) collective-permute-start(bf16[2,112,256]{2,1,0:T(8,128)(2,1)S(1)} %collective-permute-done.13), channel_id=1, source_target_pairs={{8,12},{9,13},{10,14},{11,15},{24,28},{25,29},{26,30},{27,31}} | collective-permute-start | bytes 344072 | tf_op jit(solution)/shard_map/ppermute | solution.py:66
  34.7 0.0 collective-permute-done.4
  34.7 0.7 %collective-permute-start.5 = (bf16[2,112,256]{2,1,0:T(8,128)(2,1)S(1)}, bf16[2,112,256]{2,1,0:T(8,128)(2,1)S(1)}, u32[]{:S(2)}, u32[]{:S(2)}) collective-permute-start(bf16[2,112,256]{2,1,0:T(8,128)(2,1)S(1)} %collective-permute-done.4), channel_id=1, source_target_pairs={{8,12},{9,13},{10,14},{11,15},{24,28},{25,29},{26,30},{27,31}} | collective-permute-start | bytes 344072 | tf_op jit(solution)/shard_map/ppermute | solution.py:66
  35.4 0.3 collective-permute-done.10
  35.6 1.3 %collective-permute-start.11 = (bf16[2,112,256]{2,1,0:T(8,128)(2,1)S(1)}, bf16[2,112,256]{2,1,0:T(8,128)(2,1)S(1)}, u32[]{:S(2)}, u32[]{:S(2)}) collective-permute-start(bf16[2,112,256]{2,1,0:T(8,128)(2,1)S(1)} %collective-permute-done.10), channel_id=1, source_target_pairs={{4,0},{5,1},{6,2},{7,3},{20,16},{21,17},{22,18},{23,19}} | collective-permute-start | bytes 344072 | tf_op jit(solution)/shard_map/ppermute | solution.py:67
  36.9 2.4 %collective-permute-done.1 = bf16[2,112,256]{2,1,0:T(8,128)(2,1)S(1)} collective-permute-done((bf16[2,112,256]{2,1,0:T(8,128)(2,1)S(1)}, bf16[2,112,256]{2,1,0:T(8,128)(2,1)S(1)}, u32[]{:S(2)}, u32[]{:S(2)}) %collective-permute-start.1) | collective-permute-done | bytes 114720 | tf_op jit(solution)/shard_map/ppermute | solution.py:65
  39.4 1.3 %collective-permute-start.2 = (bf16[2,112,256]{2,1,0:T(8,128)(2,1)S(1)}, bf16[2,112,256]{2,1,0:T(8,128)(2,1)S(1)}, u32[]{:S(2)}, u32[]{:S(2)}) collective-permute-start(bf16[2,112,256]{2,1,0:T(8,128)(2,1)S(1)} %collective-permute-done.1), channel_id=1, source_target_pairs={{4,0},{5,1},{6,2},{7,3},{20,16},{21,17},{22,18},{23,19}} | collective-permute-start | bytes 344072 | tf_op jit(solution)/shard_map/ppermute | solution.py:67
  40.7 0.0 collective-permute-done.14
  40.7 0.0 collective-permute-done.5
  40.7 2.0 %collective-permute-done.11 = bf16[2,112,256]{2,1,0:T(8,128)(2,1)S(1)} collective-permute-done((bf16[2,112,256]{2,1,0:T(8,128)(2,1)S(1)}, bf16[2,112,256]{2,1,0:T(8,128)(2,1)S(1)}, u32[]{:S(2)}, u32[]{:S(2)}) %collective-permute-start.11) | collective-permute-done | bytes 114720 | tf_op jit(solution)/shard_map/ppermute | solution.py:67
  42.7 0.8 %conditional.7 = (bf16[2,256,256]{2,1,0:T(8,128)(2,1)S(1)}) conditional(s32[]{:T(128)} %clamp.4, (bf16[2,2,112,256]{3,2,1,0:T(8,128)(2,1)S(1)}, bf16[2,112,256]{2,1,0:T(8,128)(2,1)S(1)}, bf16[2,112,256]{2,1,0:T(8,128)(2,1)S(1)}, bf16[2,112,256]{2,1,0:T(8,128)(2,1)S(1)}, ...), branch_computations={%region_4.5_spmd, %region_5.6_spmd, %region_6.7_spmd, %region_7.8_... | conditional | flops 237109248 | bytes 5013512
  42.7 0.5 convolution_bitcast_fusion.4
  43.3 0.1 copy.101
  43.5 0.1 collective-permute-start.17
  43.5 1.6 %collective-permute-start.16 = (bf16[1,2,64,256]{3,2,1,0:T(8,128)(2,1)S(1)}, bf16[1,2,64,256]{3,2,1,0:T(8,128)(2,1)S(1)}, u32[]{:S(2)}, u32[]{:S(2)}) collective-permute-start(bf16[1,2,64,256]{3,2,1,0:T(8,128)(2,1)S(1)} %get-tuple-element.209), channel_id=1, source_target_pairs={{0,2},{1,3},{2,0},{3,1},{4,6},{5,7},{6,4},{7,5},{8,10},{9,11},{10,... | collective-permute-start | bytes 196616 | tf_op jit(solution)/shard_map/ppermute | solution.py:23
  45.1 0.3 collective-permute-start.15
  45.4 0.6 %collective-permute-done.2 = bf16[2,112,256]{2,1,0:T(8,128)(2,1)S(1)} collective-permute-done((bf16[2,112,256]{2,1,0:T(8,128)(2,1)S(1)}, bf16[2,112,256]{2,1,0:T(8,128)(2,1)S(1)}, u32[]{:S(2)}, u32[]{:S(2)}) %collective-permute-start.2) | collective-permute-done | bytes 114720 | tf_op jit(solution)/shard_map/ppermute | solution.py:67
  46.0 0.7 %conditional.6 = (bf16[2,256,256]{2,1,0:T(8,128)(2,1)S(1)}) conditional(s32[]{:T(128)} %clamp.4, (bf16[2,2,112,256]{3,2,0,1:T(8,128)(2,1)S(1)}, bf16[2,112,256]{2,1,0:T(8,128)(2,1)S(1)}, bf16[2,112,256]{2,1,0:T(8,128)(2,1)S(1)}, bf16[2,112,256]{2,1,0:T(8,128)(2,1)S(1)}, ...), branch_computations={%region_0.1_spmd, %region_1.2_spmd, %region_2.3_spmd, %region_3.4_... | conditional | flops 237109248 | bytes 4554760
  46.1 0.5 convolution_bitcast_fusion
  46.6 0.1 copy.97
  46.8 0.5 collective-permute-start.8
  47.3 1.1 %collective-permute-start.7 = (bf16[1,2,64,256]{3,2,1,0:T(8,128)(2,1)S(1)}, bf16[1,2,64,256]{3,2,1,0:T(8,128)(2,1)S(1)}, u32[]{:S(2)}, u32[]{:S(2)}) collective-permute-start(bf16[1,2,64,256]{3,2,1,0:T(8,128)(2,1)S(1)} %get-tuple-element.206), channel_id=1, source_target_pairs={{0,2},{1,3},{2,0},{3,1},{4,6},{5,7},{6,4},{7,5},{8,10},{9,11},{10,... | collective-permute-start | bytes 196616 | tf_op jit(solution)/shard_map/ppermute | solution.py:23
  48.6 0.4 collective-permute-start.6
  48.9 1.0 %collective-permute-done.6 = bf16[1,2,64,256]{3,2,1,0:T(8,128)(2,1)S(1)} collective-permute-done((bf16[1,2,64,256]{3,2,1,0:T(8,128)(2,1)S(1)}, bf16[1,2,64,256]{3,2,1,0:T(8,128)(2,1)S(1)}, u32[]{:S(2)}, u32[]{:S(2)}) %collective-permute-start.6) | collective-permute-done | bytes 65568 | tf_op jit(solution)/shard_map/ppermute | solution.py:23
  49.9 2.8 %collective-permute-done.7 = bf16[1,2,64,256]{3,2,1,0:T(8,128)(2,1)S(1)} collective-permute-done((bf16[1,2,64,256]{3,2,1,0:T(8,128)(2,1)S(1)}, bf16[1,2,64,256]{3,2,1,0:T(8,128)(2,1)S(1)}, u32[]{:S(2)}, u32[]{:S(2)}) %collective-permute-start.7) | collective-permute-done | bytes 65568 | tf_op jit(solution)/shard_map/ppermute | solution.py:23
  52.8 0.1 maximum_convert_fusion
  52.9 0.1 slice_bitcast_fusion.29
  53.0 4.3 %multiply_select_fusion = f32[64,32,512]{2,1,0:T(8,128)} fusion(f32[32]{0:T(128)S(1)} %get-tuple-element.216, f32[64,512]{1,0:T(8,128)S(1)} %get-tuple-element.194, f32[32]{0:T(128)S(1)} %get-tuple-element.217, f32[64,512]{1,0:T(8,128)S(1)} %get-tuple-element.195, f32[32]{0:T(128)S(1)} %get-tuple-element.218, f32[64,512]{1,0:T(8,128)S(1)} %get-tuple-element.196, ...), kind=kLoop, calls=%fused_computation.152 | loop fusion | flops 20971520 | bytes 5506048 | tf_op jit(solution)/shard_map/jit(_where)/select_n | solution.py:123
  (42 shorter events, 0.6 us)
Async XLA Ops:
  0.0 1.0 %copy-start = (bf16[1,1,2,2,112,512]{5,4,3,2,1,0:T(8,128)(2,1)S(1)}, bf16[1,1,2,2,112,512]{5,4,3,2,1,0:T(8,128)(2,1)}, u32[]{:S(2)}) copy-start(bf16[1,1,2,2,112,512]{5,4,3,2,1,0:T(8,128)(2,1)} %param.14) | copy-start | bytes 1376260
  0.0 13.5 %copy-start.2 = (s32[2,64,512]{2,1,0:T(8,128)S(1)}, s32[2,64,512]{2,1,0:T(8,128)}, u32[]{:S(2)}) copy-start(s32[2,64,512]{2,1,0:T(8,128)} %param.17) | copy-start | bytes 786436
  0.0 13.6 %copy-start.1 = (bf16[1,4,2,112,256]{4,3,2,1,0:T(8,128)(2,1)S(1)}, bf16[1,4,2,112,256]{4,3,2,1,0:T(8,128)(2,1)}, u32[]{:S(2)}) copy-start(bf16[1,4,2,112,256]{4,3,2,1,0:T(8,128)(2,1)} %param.15) | copy-start | bytes 1376260
  4.9 16.5 %collective-permute-start.3 = (bf16[2,112,256]{2,1,0:T(8,128)(2,1)S(1)}, bf16[2,112,256]{2,1,0:T(8,128)(2,1)S(1)}, u32[]{:S(2)}, u32[]{:S(2)}) collective-permute-start(bf16[2,112,256]{2,1,0:T(8,128)(2,1)S(1)} %fusion.130), channel_id=1, source_target_pairs={{0,4},{4,8},{8,12},{1,5},{5,9},{9,13},{2,6},{6,10},{10,14},{3,7},{... | collective-permute-start | bytes 344072 | tf_op jit(solution)/shard_map/ppermute | solution.py:62
  9.9 5.8 %collective-permute-start.12 = (bf16[2,112,256]{2,1,0:T(8,128)(2,1)S(1)}, bf16[2,112,256]{2,1,0:T(8,128)(2,1)S(1)}, u32[]{:S(2)}, u32[]{:S(2)}) collective-permute-start(bf16[2,112,256]{2,1,0:T(8,128)(2,1)S(1)} %fusion.126), channel_id=1, source_target_pairs={{0,4},{4,8},{8,12},{1,5},{5,9},{9,13},{2,6},{6,10},{10,14},{3,7},{... | collective-permute-start | bytes 344072 | tf_op jit(solution)/shard_map/ppermute | solution.py:62
  15.7 18.2 %collective-permute-start.13 = (bf16[2,112,256]{2,1,0:T(8,128)(2,1)S(1)}, bf16[2,112,256]{2,1,0:T(8,128)(2,1)S(1)}, u32[]{:S(2)}, u32[]{:S(2)}) collective-permute-start(bf16[2,112,256]{2,1,0:T(8,128)(2,1)S(1)} %get-tuple-element.191), channel_id=1, source_target_pairs={{0,4},{4,8},{8,12},{1,5},{5,9},{9,13},{2,6},{6,10},{10,14},{3,7},{... | collective-permute-start | bytes 344072 | tf_op jit(solution)/shard_map/ppermute | solution.py:64
  20.1 7.2 %collective-permute-start.9 = (bf16[2,112,256]{2,1,0:T(8,128)(2,1)S(1)}, bf16[2,112,256]{2,1,0:T(8,128)(2,1)S(1)}, u32[]{:S(2)}, u32[]{:S(2)}) collective-permute-start(bf16[2,112,256]{2,1,0:T(8,128)(2,1)S(1)} %get-tuple-element.192), channel_id=1, source_target_pairs={{4,0},{8,4},{12,8},{5,1},{9,5},{13,9},{6,2},{10,6},{14,10},{7,3},{... | collective-permute-start | bytes 344072 | tf_op jit(solution)/shard_map/ppermute | solution.py:63
  21.4 13.3 %collective-permute-start.4 = (bf16[2,112,256]{2,1,0:T(8,128)(2,1)S(1)}, bf16[2,112,256]{2,1,0:T(8,128)(2,1)S(1)}, u32[]{:S(2)}, u32[]{:S(2)}) collective-permute-start(bf16[2,112,256]{2,1,0:T(8,128)(2,1)S(1)} %get-tuple-element.189), channel_id=1, source_target_pairs={{0,4},{4,8},{8,12},{1,5},{5,9},{9,13},{2,6},{6,10},{10,14},{3,7},{... | collective-permute-start | bytes 344072 | tf_op jit(solution)/shard_map/ppermute | solution.py:64
  26.0 6.7 %collective-permute-start = (bf16[2,112,256]{2,1,0:T(8,128)(2,1)S(1)}, bf16[2,112,256]{2,1,0:T(8,128)(2,1)S(1)}, u32[]{:S(2)}, u32[]{:S(2)}) collective-permute-start(bf16[2,112,256]{2,1,0:T(8,128)(2,1)S(1)} %get-tuple-element.190), channel_id=1, source_target_pairs={{4,0},{8,4},{12,8},{5,1},{9,5},{13,9},{6,2},{10,6},{14,10},{7,3},{... | collective-permute-start | bytes 344072 | tf_op jit(solution)/shard_map/ppermute | solution.py:63
  27.3 8.3 %collective-permute-start.10 = (bf16[2,112,256]{2,1,0:T(8,128)(2,1)S(1)}, bf16[2,112,256]{2,1,0:T(8,128)(2,1)S(1)}, u32[]{:S(2)}, u32[]{:S(2)}) collective-permute-start(bf16[2,112,256]{2,1,0:T(8,128)(2,1)S(1)} %broadcast_select_fusion.2), channel_id=1, source_target_pairs={{4,0},{8,4},{12,8},{5,1},{9,5},{13,9},{6,2},{10,6},{14,10},{7,3},{... | collective-permute-start | bytes 344072 | tf_op jit(solution)/shard_map/ppermute | solution.py:65
  32.7 6.7 %collective-permute-start.1 = (bf16[2,112,256]{2,1,0:T(8,128)(2,1)S(1)}, bf16[2,112,256]{2,1,0:T(8,128)(2,1)S(1)}, u32[]{:S(2)}, u32[]{:S(2)}) collective-permute-start(bf16[2,112,256]{2,1,0:T(8,128)(2,1)S(1)} %broadcast_select_fusion.3), channel_id=1, source_target_pairs={{4,0},{8,4},{12,8},{5,1},{9,5},{13,9},{6,2},{10,6},{14,10},{7,3},{... | collective-permute-start | bytes 344072 | tf_op jit(solution)/shard_map/ppermute | solution.py:65
  34.0 6.7 %collective-permute-start.14 = (bf16[2,112,256]{2,1,0:T(8,128)(2,1)S(1)}, bf16[2,112,256]{2,1,0:T(8,128)(2,1)S(1)}, u32[]{:S(2)}, u32[]{:S(2)}) collective-permute-start(bf16[2,112,256]{2,1,0:T(8,128)(2,1)S(1)} %collective-permute-done.13), channel_id=1, source_target_pairs={{8,12},{9,13},{10,14},{11,15},{24,28},{25,29},{26,30},{27,31}} | collective-permute-start | bytes 344072 | tf_op jit(solution)/shard_map/ppermute | solution.py:66
  34.7 6.0 %collective-permute-start.5 = (bf16[2,112,256]{2,1,0:T(8,128)(2,1)S(1)}, bf16[2,112,256]{2,1,0:T(8,128)(2,1)S(1)}, u32[]{:S(2)}, u32[]{:S(2)}) collective-permute-start(bf16[2,112,256]{2,1,0:T(8,128)(2,1)S(1)} %collective-permute-done.4), channel_id=1, source_target_pairs={{8,12},{9,13},{10,14},{11,15},{24,28},{25,29},{26,30},{27,31}} | collective-permute-start | bytes 344072 | tf_op jit(solution)/shard_map/ppermute | solution.py:66
  35.6 7.0 %collective-permute-start.11 = (bf16[2,112,256]{2,1,0:T(8,128)(2,1)S(1)}, bf16[2,112,256]{2,1,0:T(8,128)(2,1)S(1)}, u32[]{:S(2)}, u32[]{:S(2)}) collective-permute-start(bf16[2,112,256]{2,1,0:T(8,128)(2,1)S(1)} %collective-permute-done.10), channel_id=1, source_target_pairs={{4,0},{5,1},{6,2},{7,3},{20,16},{21,17},{22,18},{23,19}} | collective-permute-start | bytes 344072 | tf_op jit(solution)/shard_map/ppermute | solution.py:67
  39.4 6.7 %collective-permute-start.2 = (bf16[2,112,256]{2,1,0:T(8,128)(2,1)S(1)}, bf16[2,112,256]{2,1,0:T(8,128)(2,1)S(1)}, u32[]{:S(2)}, u32[]{:S(2)}) collective-permute-start(bf16[2,112,256]{2,1,0:T(8,128)(2,1)S(1)} %collective-permute-done.1), channel_id=1, source_target_pairs={{4,0},{5,1},{6,2},{7,3},{20,16},{21,17},{22,18},{23,19}} | collective-permute-start | bytes 344072 | tf_op jit(solution)/shard_map/ppermute | solution.py:67
  43.5 9.2 %collective-permute-start.17 = (bf16[1,2,64,256]{3,2,1,0:T(8,128)(2,1)S(1)}, bf16[1,2,64,256]{3,2,1,0:T(8,128)(2,1)S(1)}, u32[]{:S(2)}, u32[]{:S(2)}) collective-permute-start(bf16[1,2,64,256]{3,2,1,0:T(8,128)(2,1)S(1)} %get-tuple-element.208), channel_id=1, source_target_pairs={{0,3},{1,2},{2,1},{3,0},{4,7},{5,6},{6,5},{7,4},{8,11},{9,10},{10,... | collective-permute-start | bytes 196616 | tf_op jit(solution)/shard_map/ppermute | solution.py:23
  43.5 6.3 %collective-permute-start.16 = (bf16[1,2,64,256]{3,2,1,0:T(8,128)(2,1)S(1)}, bf16[1,2,64,256]{3,2,1,0:T(8,128)(2,1)S(1)}, u32[]{:S(2)}, u32[]{:S(2)}) collective-permute-start(bf16[1,2,64,256]{3,2,1,0:T(8,128)(2,1)S(1)} %get-tuple-element.209), channel_id=1, source_target_pairs={{0,2},{1,3},{2,0},{3,1},{4,6},{5,7},{6,4},{7,5},{8,10},{9,11},{10,... | collective-permute-start | bytes 196616 | tf_op jit(solution)/shard_map/ppermute | solution.py:23
  45.1 3.4 %collective-permute-start.15 = (bf16[1,2,64,256]{3,2,1,0:T(8,128)(2,1)S(1)}, bf16[1,2,64,256]{3,2,1,0:T(8,128)(2,1)S(1)}, u32[]{:S(2)}, u32[]{:S(2)}) collective-permute-start(bf16[1,2,64,256]{3,2,1,0:T(8,128)(2,1)S(1)} %get-tuple-element.210), channel_id=1, source_target_pairs={{0,1},{1,0},{2,3},{3,2},{4,5},{5,4},{6,7},{7,6},{8,9},{9,8},{10,11... | collective-permute-start | bytes 196616 | tf_op jit(solution)/shard_map/ppermute | solution.py:23
  46.8 5.9 %collective-permute-start.8 = (bf16[1,2,64,256]{3,2,1,0:T(8,128)(2,1)S(1)}, bf16[1,2,64,256]{3,2,1,0:T(8,128)(2,1)S(1)}, u32[]{:S(2)}, u32[]{:S(2)}) collective-permute-start(bf16[1,2,64,256]{3,2,1,0:T(8,128)(2,1)S(1)} %get-tuple-element.205), channel_id=1, source_target_pairs={{0,3},{1,2},{2,1},{3,0},{4,7},{5,6},{6,5},{7,4},{8,11},{9,10},{10,... | collective-permute-start | bytes 196616 | tf_op jit(solution)/shard_map/ppermute | solution.py:23
  47.3 5.3 %collective-permute-start.7 = (bf16[1,2,64,256]{3,2,1,0:T(8,128)(2,1)S(1)}, bf16[1,2,64,256]{3,2,1,0:T(8,128)(2,1)S(1)}, u32[]{:S(2)}, u32[]{:S(2)}) collective-permute-start(bf16[1,2,64,256]{3,2,1,0:T(8,128)(2,1)S(1)} %get-tuple-element.206), channel_id=1, source_target_pairs={{0,2},{1,3},{2,0},{3,1},{4,6},{5,7},{6,4},{7,5},{8,10},{9,11},{10,... | collective-permute-start | bytes 196616 | tf_op jit(solution)/shard_map/ppermute | solution.py:23
  48.6 1.3 %collective-permute-start.6 = (bf16[1,2,64,256]{3,2,1,0:T(8,128)(2,1)S(1)}, bf16[1,2,64,256]{3,2,1,0:T(8,128)(2,1)S(1)}, u32[]{:S(2)}, u32[]{:S(2)}) collective-permute-start(bf16[1,2,64,256]{3,2,1,0:T(8,128)(2,1)S(1)} %get-tuple-element.207), channel_id=1, source_target_pairs={{0,1},{1,0},{2,3},{3,2},{4,5},{5,4},{6,7},{7,6},{8,9},{9,8},{10,11... | collective-permute-start | bytes 196616 | tf_op jit(solution)/shard_map/ppermute | solution.py:23
